TPU v7x, 512 devices: a whole 4x4x16 slice. The times are simulated.
512 devices in a mesh: tok: 64 (over z, x), head: 8 (over y, core).
Axes of the slice: x: 4, y: 4, z: 16, core: 2. Of those that a mesh axis runs over, the one named last changes fastest.
Arguments:
- tokens: bfloat16 [32768, 2560], P('tok', 'head'), may hold values from -6 to 6
- query_weight: bfloat16 [2560, 2560], P('tok'), may hold values from -0.125 to 0.125
- keyvalue_weight: bfloat16 [2560, 512], P('tok'), may hold values from -0.125 to 0.125
- output_weight: bfloat16 [2560, 2560], P(None, ('head', 'tok')), may hold values from -0.125 to 0.125
- cache: bfloat16 [2048, 2, 128, 256], P(('tok', 'head')), may hold values from -460 to 460
- page_table: int32 [512, 4], P('tok'), may hold values from 0 to 2047, as said below
- parents: int32 [512, 64], P('tok'), may hold values from 0 to 62, as said below
- cache_len: int32 [512], P('tok'), may hold values from 1 to 448, as said below
- accepted_leaf: int32 [512], P('tok'), may hold values from 0 to 63
Outputs:
- attended: bfloat16 [32768, 2560], P('tok', 'head')
- cache_out: bfloat16 [2048, 2, 128, 256], P(('tok', 'head'))
Inputs may be any that keep to these rules, and one draw needn't show every extreme that they name: `page_table`: for every d, row d names each of the pages d * 4 to d * 4 + 3 exactly once, so request d's pages all lie on device d (devices counted tok-major, head-minor). parents[r, 0] = 0, and parents[r, i] < i for i >= 1. `cache_len`: roughly half of the requests hold at most 128 cached positions, the others more than 320.
All inputs are finite; a program needn't handle non-finite values.
Results may differ from a plain program's by a relative error of at most 0.014.
The roundings to bfloat16 on the way count: a program that leaves them out, or rounds other values in their place, can miss the bound.
Values may be sent and summed in bfloat16 or wider, within the bound.
No kernel may reach another device: no remote copies, remote signals or barrier semaphores. Data moves between devices by JAX's collectives and lax.ppermute only.
A program may use at most 64 MiB of HBM per device.

v0:
```python
import math
import jax
import jax.numpy as jnp
from jax import lax
from jax.sharding import Mesh, PartitionSpec as P

HQ = 10
HD = 256
DRAFT = 64
PAGE = 128
NPR = 4
WINDOW = 256


def ancestry(parent_row):
    node_ids = jnp.arange(DRAFT, dtype=jnp.int32)
    link = (parent_row[:, None] == node_ids[None, :]).astype(jnp.float32)
    reach = jnp.minimum(link + jnp.eye(DRAFT, dtype=jnp.float32), 1.0)
    for sweep in range((DRAFT - 1).bit_length()):
        reach = jnp.minimum(jnp.dot(reach, reach, precision=lax.Precision.HIGHEST), 1.0)
    depth = (jnp.sum(reach, axis=1) - 1.0).astype(jnp.int32)
    return (reach, depth)


def rotate(values, position):
    half = HD // 4
    freq = jnp.exp(jnp.arange(half, dtype=jnp.float32) * (-2.0 * math.log(10000.0) / (HD // 2)))
    angle = position.astype(jnp.float32)[..., None] * freq
    cosine = jnp.cos(angle)
    sine = jnp.sin(angle)
    first = values[..., :half]
    second = values[..., half : 2 * half]
    return jnp.concatenate(
        [first * cosine - second * sine, second * cosine + first * sine, values[..., 2 * half :]],
        axis=-1,
    )


def attend(queries, cache_keys, cache_values, tree_keys, tree_values, lengths, position, reach):
    window_span = cache_keys.shape[1]
    slot_ids = jnp.arange(window_span, dtype=jnp.int32)
    visible = (slot_ids[None, None, :] < lengths[:, None, None]) & (
        slot_ids[None, None, :] > position[:, :, None] - WINDOW
    )
    cache_scores = jnp.einsum(
        "rnhd,rcd->rhnc", queries, cache_keys, preferred_element_type=jnp.float32
    )
    tree_scores = jnp.einsum(
        "rnhd,rmd->rhnm", queries, tree_keys, preferred_element_type=jnp.float32
    )
    cache_scores = jnp.where(visible[:, None], cache_scores, -1e30)
    tree_scores = jnp.where(reach[:, None] > 0.5, tree_scores, -1e30)
    row_peak = jnp.maximum(jnp.max(cache_scores, axis=-1), jnp.max(tree_scores, axis=-1))[..., None]
    cache_weights = jnp.exp(cache_scores - row_peak)
    tree_weights = jnp.exp(tree_scores - row_peak)
    denominator = jnp.sum(cache_weights, axis=-1, keepdims=True) + jnp.sum(
        tree_weights, axis=-1, keepdims=True
    )
    cache_weights = (cache_weights / denominator).astype(jnp.bfloat16)
    tree_weights = (tree_weights / denominator).astype(jnp.bfloat16)
    result = jnp.einsum(
        "rhnc,rcd->rhnd", cache_weights, cache_values, preferred_element_type=jnp.float32
    )
    result = result + jnp.einsum(
        "rhnm,rmd->rhnd", tree_weights, tree_values, preferred_element_type=jnp.float32
    )
    return result.astype(jnp.bfloat16)


def refresh(logical_pages, length, leaf, reach, depth, new_keys, new_values):
    count = logical_pages.shape[0] * logical_pages.shape[2]
    logical = jnp.transpose(logical_pages, (1, 0, 2, 3)).reshape(2, count, HD)
    slot_ids = jnp.arange(count, dtype=jnp.int32)
    on_path = reach[leaf]
    selector = ((on_path[None, :] > 0.5) & (depth[None, :] == slot_ids[:, None] - length)).astype(
        jnp.float32
    )
    placed_keys = jnp.dot(selector, new_keys.astype(jnp.float32), precision=lax.Precision.HIGHEST)
    placed_values = jnp.dot(
        selector, new_values.astype(jnp.float32), precision=lax.Precision.HIGHEST
    )
    placed = jnp.stack([placed_keys, placed_values]).astype(jnp.bfloat16)
    written = jnp.sum(selector, axis=1) > 0.5
    logical = jnp.where(written[None, :, None], placed, logical)
    return jnp.transpose(
        logical.reshape(2, logical_pages.shape[0], logical_pages.shape[2], HD), (1, 0, 2, 3)
    )


def ring_pieces(piece, axis):
    size = lax.axis_size(axis)
    got = [(0, 0, piece)]
    ahead = piece
    behind = piece
    forward = [(i, (i + 1) % size) for i in range(size)]
    backward = [(i, (i - 1) % size) for i in range(size)]
    for step in range(1, size // 2 + 1):
        if 2 * step == size and size > 2:
            half = piece.shape[0] // 2
            got.append((step, 0, lax.ppermute(ahead[:half], axis, forward)))
            got.append((step, half, lax.ppermute(behind[half:], axis, backward)))
            break
        ahead = lax.ppermute(ahead, axis, forward)
        got.append((size - step, 0, ahead))
        if step <= (size - 1) // 2:
            behind = lax.ppermute(behind, axis, backward)
            got.append((step, 0, behind))
    return got


def grid_gather(piece):
    z_size = lax.axis_size("tz")
    x_size = lax.axis_size("tx")
    z_index = lax.axis_index("tz")
    x_index = lax.axis_index("tx")
    zero = jnp.int32(0)
    column = jnp.zeros((z_size,) + piece.shape, piece.dtype)
    for offset, first, part in ring_pieces(piece, "tz"):
        column = lax.dynamic_update_slice(
            column, part[None], ((z_index + offset) % z_size, jnp.int32(first), zero)
        )
    placed = jnp.zeros((z_size, x_size) + piece.shape, piece.dtype)
    for offset, first, part in ring_pieces(column, "tx"):
        placed = lax.dynamic_update_slice(
            placed, part[:, None], (jnp.int32(first), (x_index + offset) % x_size, zero, zero)
        )
    return placed.reshape((z_size * x_size,) + piece.shape)


def shards(
    tokens,
    query_weight,
    keyvalue_weight,
    output_weight,
    cache,
    page_table,
    parents,
    cache_len,
    accepted_leaf,
):
    head_count = lax.axis_size("head")
    head_index = lax.axis_index("head")
    tok_index = lax.axis_index("tz") * lax.axis_size("tx") + lax.axis_index("tx")
    requests = parents.shape[0]
    assert requests == head_count
    pages_dev = cache.shape[0]
    part_rows = query_weight.shape[0]
    q_cols = HQ * HD // head_count
    kv_cols = 2 * HD // head_count
    out_cols = output_weight.shape[1]
    wq_piece = lax.dynamic_slice_in_dim(query_weight, head_index * q_cols, q_cols, axis=1)
    wkv_piece = lax.dynamic_slice_in_dim(keyvalue_weight, head_index * kv_cols, kv_cols, axis=1)
    proj_piece = jnp.concatenate([wq_piece, wkv_piece], axis=1)
    width = proj_piece.shape[1]
    wo_flat = output_weight.reshape(-1)
    wo_rows = -(-wo_flat.shape[0] // width)
    wo_rows = -(-(part_rows + wo_rows) // 8) * 8 - part_rows
    wo_block = jnp.pad(wo_flat, (0, wo_rows * width - wo_flat.shape[0])).reshape(wo_rows, width)
    piece = jnp.concatenate([proj_piece, wo_block], axis=0)
    stacked = grid_gather(piece)
    tok_count = stacked.shape[0]
    proj_w = stacked[:, :part_rows].reshape(tok_count * part_rows, width)
    wo_cols = (
        stacked[:, part_rows:]
        .reshape(tok_count, -1)[:, : wo_flat.shape[0]]
        .reshape(tok_count, HQ * HD, out_cols)
        .transpose(1, 0, 2)
        .reshape(HQ * HD, tok_count * out_cols)
    )
    gathered = lax.all_gather(tokens, "head", axis=1, tiled=True)
    wide = gathered.astype(jnp.float32)
    mean_square = jnp.mean(wide * wide, axis=1, keepdims=True)
    normed = (wide * lax.rsqrt(mean_square + 1e-06)).astype(jnp.bfloat16)
    both = jnp.dot(normed, proj_w, preferred_element_type=jnp.float32)
    mine = lax.all_to_all(both, "head", 0, 1, tiled=True)
    mine = mine.reshape(DRAFT, head_count, q_cols + kv_cols)
    q_pre = mine[:, :, :q_cols].reshape(DRAFT, HQ, HD)
    kv_pre = mine[:, :, q_cols:].reshape(DRAFT, 2 * HD)
    parent_row = lax.dynamic_index_in_dim(parents, head_index, 0, keepdims=False)
    length = lax.dynamic_index_in_dim(cache_len, head_index, 0, keepdims=False)
    leaf = lax.dynamic_index_in_dim(accepted_leaf, head_index, 0, keepdims=False)
    reach, depth = ancestry(parent_row)
    position = length + depth
    queries = (rotate(q_pre, position[:, None]) * HD ** (-0.5)).astype(jnp.bfloat16)
    tree_keys = rotate(kv_pre[:, :HD], position).astype(jnp.bfloat16)
    tree_values = kv_pre[:, HD:].astype(jnp.bfloat16)
    device = tok_index * head_count + head_index
    own_table = (
        lax.dynamic_index_in_dim(page_table, head_index, 0, keepdims=False) - device * pages_dev
    )
    own_pages = jnp.take(cache, own_table, axis=0)
    cache_keys = own_pages[:, 0].reshape(NPR * PAGE, HD)
    cache_values = own_pages[:, 1].reshape(NPR * PAGE, HD)
    result = attend(
        queries[None],
        cache_keys[None],
        cache_values[None],
        tree_keys[None],
        tree_values[None],
        length[None],
        position[None],
        reach[None],
    )
    mixed = lax.all_gather(result[0], "head", axis=1, tiled=True)
    per_head = lax.dot_general(
        mixed,
        wo_cols.reshape(HQ, HD, wo_cols.shape[1]),
        (((2,), (1,)), ((0,), (0,))),
        preferred_element_type=jnp.float32,
    )
    summed = None
    for group in range(head_count):
        head_ids = [k for k in range(group, HQ, head_count)]
        if not head_ids:
            continue
        partial_value = per_head[head_ids[0]]
        for k in head_ids[1:]:
            partial_value = partial_value + per_head[k]
        term = partial_value.astype(jnp.bfloat16).astype(jnp.float32)
        summed = term if summed is None else summed + term
    attended = summed.astype(jnp.bfloat16)
    new_pages = refresh(own_pages, length, leaf, reach, depth, tree_keys, tree_values)
    matches = (own_table[:, None] == jnp.arange(pages_dev, dtype=jnp.int32)[None, :]).astype(
        jnp.int32
    )
    inverse = jnp.sum(matches * jnp.arange(pages_dev, dtype=jnp.int32)[:, None], axis=0)
    cache_out = jnp.take(new_pages, inverse, axis=0)
    return (attended, cache_out)


def solution(mesh):
    tok_size = mesh.shape["tok"]
    tx_size = 4 if tok_size % 4 == 0 else tok_size
    grid = Mesh(
        mesh.devices.reshape(tok_size // tx_size, tx_size, mesh.shape["head"]), ("tz", "tx", "head")
    )
    tok = ("tz", "tx")
    in_specs = (
        P(tok, "head"),
        P(tok, None),
        P(tok, None),
        P(None, ("head",) + tok),
        P(tok + ("head",), None, None, None),
        P(tok, None),
        P(tok, None),
        P(tok),
        P(tok),
    )
    out_specs = (P(tok, "head"), P(tok + ("head",), None, None, None))
    return jax.shard_map(shards, mesh=grid, in_specs=in_specs, out_specs=out_specs, check_vma=False)
```

profile of v0, /device:TPU:1, one launch (start us, length us, event | category | flops | bytes accessed | tf_op | source)
XLA Modules:
  0.0 198.7 jit_solution(2662571134446232722)
XLA Ops:
  7.3 1.2 copy.43
  8.5 1.0 reshape.344
  9.5 0.8 constant_dynamic-slice_fusion.1
  10.3 0.9 constant_dynamic-slice_fusion.2
  11.3 4.4 %collective-permute-start = (bf16[80,384]{1,0:T(8,128)(2,1)S(1)}, bf16[80,384]{1,0:T(8,128)(2,1)S(1)}, u32[]{:S(2)}, u32[]{:S(2)}) collective-permute-start(bf16[80,384]{1,0:T(8,128)(2,1)S(1)} %get-tuple-element.6), channel_id=1, source_target_pairs={{0,32},{32,64},{64,96},{96,128},{128,160},{160,192},{192,224},{224... | collective-permute-start | bytes 184328 | tf_op jit(solution)/shard_map/ppermute | solution.py:103
  15.7 9.5 %collective-permute-start.1 = (bf16[80,384]{1,0:T(8,128)(2,1)S(1)}, bf16[80,384]{1,0:T(8,128)(2,1)S(1)}, u32[]{:S(2)}, u32[]{:S(2)}) collective-permute-start(bf16[80,384]{1,0:T(8,128)(2,1)S(1)} %get-tuple-element.6), channel_id=1, source_target_pairs={{0,480},{32,0},{64,32},{96,64},{128,96},{160,128},{192,160},{224,1... | collective-permute-start | bytes 184328 | tf_op jit(solution)/shard_map/ppermute | solution.py:106
  27.9 0.7 fusion.38
  31.4 0.7 iota_compare_fusion.6
  32.1 1.9 collective-permute-start.2
  34.0 4.6 %collective-permute-start.3 = (bf16[80,384]{1,0:T(8,128)(2,1)S(1)}, bf16[80,384]{1,0:T(8,128)(2,1)S(1)}, u32[]{:S(2)}, u32[]{:S(2)}) collective-permute-start(bf16[80,384]{1,0:T(8,128)(2,1)S(1)} %collective-permute-done.1), channel_id=1, source_target_pairs={{0,480},{32,0},{64,32},{96,64},{128,96},{160,128},{192,160},{224,1... | collective-permute-start | bytes 184328 | tf_op jit(solution)/shard_map/ppermute | solution.py:106
  38.6 1.9 collective-permute-start.4
  40.6 4.6 %collective-permute-start.5 = (bf16[80,384]{1,0:T(8,128)(2,1)S(1)}, bf16[80,384]{1,0:T(8,128)(2,1)S(1)}, u32[]{:S(2)}, u32[]{:S(2)}) collective-permute-start(bf16[80,384]{1,0:T(8,128)(2,1)S(1)} %collective-permute-done.3), channel_id=1, source_target_pairs={{0,480},{32,0},{64,32},{96,64},{128,96},{160,128},{192,160},{224,1... | collective-permute-start | bytes 184328 | tf_op jit(solution)/shard_map/ppermute | solution.py:106
  45.2 1.9 collective-permute-start.6
  47.2 4.6 %collective-permute-start.7 = (bf16[80,384]{1,0:T(8,128)(2,1)S(1)}, bf16[80,384]{1,0:T(8,128)(2,1)S(1)}, u32[]{:S(2)}, u32[]{:S(2)}) collective-permute-start(bf16[80,384]{1,0:T(8,128)(2,1)S(1)} %collective-permute-done.5), channel_id=1, source_target_pairs={{0,480},{32,0},{64,32},{96,64},{128,96},{160,128},{192,160},{224,1... | collective-permute-start | bytes 184328 | tf_op jit(solution)/shard_map/ppermute | solution.py:106
  51.8 1.9 collective-permute-start.8
  53.7 4.6 %collective-permute-start.9 = (bf16[80,384]{1,0:T(8,128)(2,1)S(1)}, bf16[80,384]{1,0:T(8,128)(2,1)S(1)}, u32[]{:S(2)}, u32[]{:S(2)}) collective-permute-start(bf16[80,384]{1,0:T(8,128)(2,1)S(1)} %collective-permute-done.7), channel_id=1, source_target_pairs={{0,480},{32,0},{64,32},{96,64},{128,96},{160,128},{192,160},{224,1... | collective-permute-start | bytes 184328 | tf_op jit(solution)/shard_map/ppermute | solution.py:106
  58.4 1.9 collective-permute-start.10
  60.3 4.6 %collective-permute-start.11 = (bf16[80,384]{1,0:T(8,128)(2,1)S(1)}, bf16[80,384]{1,0:T(8,128)(2,1)S(1)}, u32[]{:S(2)}, u32[]{:S(2)}) collective-permute-start(bf16[80,384]{1,0:T(8,128)(2,1)S(1)} %collective-permute-done.9), channel_id=1, source_target_pairs={{0,480},{32,0},{64,32},{96,64},{128,96},{160,128},{192,160},{224,1... | collective-permute-start | bytes 184328 | tf_op jit(solution)/shard_map/ppermute | solution.py:106
  65.0 1.9 collective-permute-start.12
  66.9 4.6 %collective-permute-start.13 = (bf16[80,384]{1,0:T(8,128)(2,1)S(1)}, bf16[80,384]{1,0:T(8,128)(2,1)S(1)}, u32[]{:S(2)}, u32[]{:S(2)}) collective-permute-start(bf16[80,384]{1,0:T(8,128)(2,1)S(1)} %collective-permute-done.11), channel_id=1, source_target_pairs={{0,480},{32,0},{64,32},{96,64},{128,96},{160,128},{192,160},{224,1... | collective-permute-start | bytes 184328 | tf_op jit(solution)/shard_map/ppermute | solution.py:106
  71.6 1.9 collective-permute-start.14
  73.5 4.6 %collective-permute-start.15 = (bf16[40,384]{1,0:T(8,128)(2,1)S(1)}, bf16[40,384]{1,0:T(8,128)(2,1)S(1)}, u32[]{:S(2)}, u32[]{:S(2)}) collective-permute-start(bf16[40,384]{1,0:T(8,128)(2,1)S(1)} %slice.130), channel_id=1, source_target_pairs={{0,480},{32,0},{64,32},{96,64},{128,96},{160,128},{192,160},{224,1... | collective-permute-start | bytes 92168 | tf_op jit(solution)/shard_map/ppermute | solution.py:101
  78.2 0.9 collective-permute-done.15
  79.1 4.4 %collective-permute-start.17 = (bf16[16,80,384]{2,1,0:T(8,128)(2,1)S(1)}, bf16[16,80,384]{2,1,0:T(8,128)(2,1)S(1)}, u32[]{:S(2)}, u32[]{:S(2)}) collective-permute-start(bf16[16,80,384]{2,1,0:T(8,128)(2,1)S(1)} %bitcast_dynamic-update-slice_fusion.20), channel_id=1, source_target_pairs={{0,24},{8,0},{16,8},{24,16},{1,25},{9,1},{17,9},{25,17},{2,26},{10... | collective-permute-start | bytes 2949128 | tf_op jit(solution)/shard_map/ppermute | solution.py:106
  83.5 1.9 collective-permute-start.16
  86.5 11.6 %collective-permute-done.17 = bf16[16,80,384]{2,1,0:T(8,128)(2,1)S(1)} collective-permute-done((bf16[16,80,384]{2,1,0:T(8,128)(2,1)S(1)}, bf16[16,80,384]{2,1,0:T(8,128)(2,1)S(1)}, u32[]{:S(2)}, u32[]{:S(2)}) %collective-permute-start.17) | collective-permute-done | bytes 983072 | tf_op jit(solution)/shard_map/ppermute | solution.py:106
  98.1 5.3 %collective-permute-start.19 = (bf16[8,80,384]{2,1,0:T(8,128)(2,1)S(1)}, bf16[8,80,384]{2,1,0:T(8,128)(2,1)S(1)}, u32[]{:S(2)}, u32[]{:S(2)}) collective-permute-start(bf16[8,80,384]{2,1,0:T(8,128)(2,1)S(1)} %slice.132), channel_id=1, source_target_pairs={{0,24},{8,0},{16,8},{24,16},{1,25},{9,1},{17,9},{25,17},{2,26},{10... | collective-permute-start | bytes 1474568 | tf_op jit(solution)/shard_map/ppermute | solution.py:101
  103.5 1.9 collective-permute-start.18
  105.9 9.5 %collective-permute-done.18 = bf16[8,80,384]{2,1,0:T(8,128)(2,1)S(1)} collective-permute-done((bf16[8,80,384]{2,1,0:T(8,128)(2,1)S(1)}, bf16[8,80,384]{2,1,0:T(8,128)(2,1)S(1)}, u32[]{:S(2)}, u32[]{:S(2)}) %collective-permute-start.18) | collective-permute-done | bytes 491552 | tf_op jit(solution)/shard_map/ppermute | solution.py:100
  115.5 2.3 %fusion.44 = (bf16[64,40,384]{2,1,0:T(8,128)(2,1)}, bf16[64,40,384]{2,1,0:T(8,128)(2,1)}) fusion(bf16[64,80,384]{2,1,0:T(8,128)(2,1)S(1)} %bitcast.125), kind=kLoop, calls=%fused_computation.126 | loop fusion | bytes 7864320 | tf_op jit(solution)/shard_map/slice | solution.py:164
  117.8 3.0 %copy.42 = bf16[512,2560]{1,0:T(8,128)(2,1)S(1)} copy(bf16[512,2560]{0,1:T(8,128)(2,1)} %all-gather.3.cloned.1.call-done) | data formatting | bytes 5242880 | tf_op jit(solution)/shard_map/all_gather | solution.py:170
  121.9 1.0 copy-done.3
  123.0 2.4 %fusion.50 = f32[8,64,384]{2,1,0:T(8,128)} fusion(bf16[8,64,2560]{2,1,0:T(8,128)(2,1)S(1)} %bitcast.129, bf16[2560,384,1]{1,0,2:T(8,128)(2,1)S(1)} %bitcast.130), kind=kOutput, calls=%fused_computation.132 | convolution fusion | flops 1006632960 | bytes 5373952 | tf_op jit(solution)/shard_map/dot_general | solution.py:174
  125.4 13.3 %all-to-all-start = ((f32[8,64,384]{2,1,0:T(8,128)}), f32[8,64,384]{2,1,0:T(8,128)S(1)}, u32[]{:S(2)}, u32[]{:S(2)}) async-start(f32[8,64,384]{2,1,0:T(8,128)} %fusion.50), calls=%async_computation | async-start | bytes 1572864 | tf_op jit(solution)/shard_map/all_to_all | solution.py:175
  139.4 0.7 add_add_fusion
  140.2 10.7 %all-to-all-done = f32[8,64,384]{2,1,0:T(8,128)S(1)} async-done(((f32[8,64,384]{2,1,0:T(8,128)}), f32[8,64,384]{2,1,0:T(8,128)S(1)}, u32[]{:S(2)}, u32[]{:S(2)}) %all-to-all-start) | async-done | bytes 786464 | tf_op jit(solution)/shard_map/all_to_all | solution.py:175
  153.3 1.0 fusion.13
  156.4 1.2 fusion.5
  158.0 3.8 %copy.51 = bf16[64,40,384]{0,2,1:T(8,128)(2,1)} copy(bf16[64,40,384]{2,1,0:T(8,128)(2,1)S(1)} %copy-done.2) | data formatting | bytes 3932160 | tf_op jit(solution)/shard_map/slice | solution.py:164
  161.8 3.3 %slice.145 = bf16[64,12800]{0,1:T(8,128)(2,1)} slice(bf16[64,15360]{0,1:T(8,128)(2,1)} %bitcast.126), slice={[0:64], [0:12800]} | slice | bytes 3276800 | tf_op jit(solution)/shard_map/slice | solution.py:164
  165.1 7.1 %reshape.354 = bf16[64,2560,5]{0,2,1:T(8,128)(2,1)} reshape(bf16[64,12800]{0,1:T(8,128)(2,1)} %slice.145) | data formatting | bytes 3276800 | tf_op jit(solution)/shard_map/reshape | solution.py:166
  172.2 7.0 %copy.52 = bf16[2560,64,5]{0,2,1:T(8,128)(2,1)S(1)} copy(bf16[2560,64,5]{1,2,0:T(8,128)(2,1)} %bitcast.124) | data formatting | bytes 3276800 | tf_op jit(solution)/shard_map/transpose | solution.py:167
  179.3 3.1 %reshape_reshape.3 = bf16[10,256,320]{1,0,2:T(8,128)(2,1)} reshape(bf16[2560,64,5]{0,2,1:T(8,128)(2,1)S(1)} %copy.52) | data formatting | bytes 3276800 | tf_op jit(solution)/shard_map/reshape;reshape | solution.py:207
  182.3 1.6 gather_fusion.1
  184.0 0.9 broadcast_select_fusion
  184.9 1.8 all-gather.5.cloned.1.call-done
  186.7 4.0 %fusion.49 = (bf16[10,512,320]{1,2,0:T(8,128)(2,1)S(1)}, f32[10,512,320]{1,2,0:T(8,128)S(1)}) fusion(bf16[10,512,256]{2,1,0:T(8,128)(2,1)} %all-gather.5.cloned.1.call-done, bf16[10,256,320]{1,0,2:T(8,128)(2,1)} %reshape_reshape.3), kind=kOutput, calls=%fused_computation.131 | convolution fusion | flops 840499200 | bytes 14090240 | tf_op jit(solution)/shard_map/dot_general | solution.py:205
  190.7 1.2 fusion.14
  (115 shorter events, 12.2 us)
Async XLA Ops:
  7.2 131.6 %copy-start = (bf16[4,2,128,256]{3,2,1,0:T(8,128)(2,1)S(1)}, bf16[4,2,128,256]{3,2,1,0:T(8,128)(2,1)}, u32[]{:S(2)}) copy-start(bf16[4,2,128,256]{3,2,1,0:T(8,128)(2,1)} %param.15) | copy-start | bytes 1572868
  7.2 18.2 %copy-start.5 = (s32[8]{0:T(128)S(1)}, s32[8]{0:T(128)}, u32[]{:S(2)}) copy-start(s32[8]{0:T(128)} %param.19) | copy-start | bytes 100
  7.2 20.1 %copy-start.6 = (s32[8]{0:T(128)S(1)}, s32[8]{0:T(128)}, u32[]{:S(2)}) copy-start(s32[8]{0:T(128)} %param.18) | copy-start | bytes 100
  7.2 21.4 %copy-start.4 = (s32[8,4]{0,1:T(4,128)S(1)}, s32[8,4]{0,1:T(4,128)}, u32[]{:S(2)}) copy-start(s32[8,4]{0,1:T(4,128)} %param.16) | copy-start | bytes 388
  7.2 110.6 %all-gather.3.cloned.1.call-start = ((), (), s32[]{:S(2)}) async-start(), calls=%async_computation.1 | async-start | bytes 2949120 | tf_op jit(solution)/shard_map/all_gather | solution.py:170
  11.3 20.7 %collective-permute-start = (bf16[80,384]{1,0:T(8,128)(2,1)S(1)}, bf16[80,384]{1,0:T(8,128)(2,1)S(1)}, u32[]{:S(2)}, u32[]{:S(2)}) collective-permute-start(bf16[80,384]{1,0:T(8,128)(2,1)S(1)} %get-tuple-element.6), channel_id=1, source_target_pairs={{0,32},{32,64},{64,96},{96,128},{128,160},{160,192},{192,224},{224... | collective-permute-start | bytes 184328 | tf_op jit(solution)/shard_map/ppermute | solution.py:103
  15.7 18.3 %collective-permute-start.1 = (bf16[80,384]{1,0:T(8,128)(2,1)S(1)}, bf16[80,384]{1,0:T(8,128)(2,1)S(1)}, u32[]{:S(2)}, u32[]{:S(2)}) collective-permute-start(bf16[80,384]{1,0:T(8,128)(2,1)S(1)} %get-tuple-element.6), channel_id=1, source_target_pairs={{0,480},{32,0},{64,32},{96,64},{128,96},{160,128},{192,160},{224,1... | collective-permute-start | bytes 184328 | tf_op jit(solution)/shard_map/ppermute | solution.py:106
  32.1 6.6 %collective-permute-start.2 = (bf16[80,384]{1,0:T(8,128)(2,1)S(1)}, bf16[80,384]{1,0:T(8,128)(2,1)S(1)}, u32[]{:S(2)}, u32[]{:S(2)}) collective-permute-start(bf16[80,384]{1,0:T(8,128)(2,1)S(1)} %collective-permute-done), channel_id=1, source_target_pairs={{0,32},{32,64},{64,96},{96,128},{128,160},{160,192},{192,224},{224... | collective-permute-start | bytes 184328 | tf_op jit(solution)/shard_map/ppermute | solution.py:103
  34.0 6.6 %collective-permute-start.3 = (bf16[80,384]{1,0:T(8,128)(2,1)S(1)}, bf16[80,384]{1,0:T(8,128)(2,1)S(1)}, u32[]{:S(2)}, u32[]{:S(2)}) collective-permute-start(bf16[80,384]{1,0:T(8,128)(2,1)S(1)} %collective-permute-done.1), channel_id=1, source_target_pairs={{0,480},{32,0},{64,32},{96,64},{128,96},{160,128},{192,160},{224,1... | collective-permute-start | bytes 184328 | tf_op jit(solution)/shard_map/ppermute | solution.py:106
  38.6 6.6 %collective-permute-start.4 = (bf16[80,384]{1,0:T(8,128)(2,1)S(1)}, bf16[80,384]{1,0:T(8,128)(2,1)S(1)}, u32[]{:S(2)}, u32[]{:S(2)}) collective-permute-start(bf16[80,384]{1,0:T(8,128)(2,1)S(1)} %collective-permute-done.2), channel_id=1, source_target_pairs={{0,32},{32,64},{64,96},{96,128},{128,160},{160,192},{192,224},{224... | collective-permute-start | bytes 184328 | tf_op jit(solution)/shard_map/ppermute | solution.py:103
  40.6 6.6 %collective-permute-start.5 = (bf16[80,384]{1,0:T(8,128)(2,1)S(1)}, bf16[80,384]{1,0:T(8,128)(2,1)S(1)}, u32[]{:S(2)}, u32[]{:S(2)}) collective-permute-start(bf16[80,384]{1,0:T(8,128)(2,1)S(1)} %collective-permute-done.3), channel_id=1, source_target_pairs={{0,480},{32,0},{64,32},{96,64},{128,96},{160,128},{192,160},{224,1... | collective-permute-start | bytes 184328 | tf_op jit(solution)/shard_map/ppermute | solution.py:106
  45.2 6.6 %collective-permute-start.6 = (bf16[80,384]{1,0:T(8,128)(2,1)S(1)}, bf16[80,384]{1,0:T(8,128)(2,1)S(1)}, u32[]{:S(2)}, u32[]{:S(2)}) collective-permute-start(bf16[80,384]{1,0:T(8,128)(2,1)S(1)} %collective-permute-done.4), channel_id=1, source_target_pairs={{0,32},{32,64},{64,96},{96,128},{128,160},{160,192},{192,224},{224... | collective-permute-start | bytes 184328 | tf_op jit(solution)/shard_map/ppermute | solution.py:103
  47.2 6.6 %collective-permute-start.7 = (bf16[80,384]{1,0:T(8,128)(2,1)S(1)}, bf16[80,384]{1,0:T(8,128)(2,1)S(1)}, u32[]{:S(2)}, u32[]{:S(2)}) collective-permute-start(bf16[80,384]{1,0:T(8,128)(2,1)S(1)} %collective-permute-done.5), channel_id=1, source_target_pairs={{0,480},{32,0},{64,32},{96,64},{128,96},{160,128},{192,160},{224,1... | collective-permute-start | bytes 184328 | tf_op jit(solution)/shard_map/ppermute | solution.py:106
  51.8 6.6 %collective-permute-start.8 = (bf16[80,384]{1,0:T(8,128)(2,1)S(1)}, bf16[80,384]{1,0:T(8,128)(2,1)S(1)}, u32[]{:S(2)}, u32[]{:S(2)}) collective-permute-start(bf16[80,384]{1,0:T(8,128)(2,1)S(1)} %collective-permute-done.6), channel_id=1, source_target_pairs={{0,32},{32,64},{64,96},{96,128},{128,160},{160,192},{192,224},{224... | collective-permute-start | bytes 184328 | tf_op jit(solution)/shard_map/ppermute | solution.py:103
  53.7 6.6 %collective-permute-start.9 = (bf16[80,384]{1,0:T(8,128)(2,1)S(1)}, bf16[80,384]{1,0:T(8,128)(2,1)S(1)}, u32[]{:S(2)}, u32[]{:S(2)}) collective-permute-start(bf16[80,384]{1,0:T(8,128)(2,1)S(1)} %collective-permute-done.7), channel_id=1, source_target_pairs={{0,480},{32,0},{64,32},{96,64},{128,96},{160,128},{192,160},{224,1... | collective-permute-start | bytes 184328 | tf_op jit(solution)/shard_map/ppermute | solution.py:106
  58.4 6.6 %collective-permute-start.10 = (bf16[80,384]{1,0:T(8,128)(2,1)S(1)}, bf16[80,384]{1,0:T(8,128)(2,1)S(1)}, u32[]{:S(2)}, u32[]{:S(2)}) collective-permute-start(bf16[80,384]{1,0:T(8,128)(2,1)S(1)} %collective-permute-done.8), channel_id=1, source_target_pairs={{0,32},{32,64},{64,96},{96,128},{128,160},{160,192},{192,224},{224... | collective-permute-start | bytes 184328 | tf_op jit(solution)/shard_map/ppermute | solution.py:103
  60.3 6.6 %collective-permute-start.11 = (bf16[80,384]{1,0:T(8,128)(2,1)S(1)}, bf16[80,384]{1,0:T(8,128)(2,1)S(1)}, u32[]{:S(2)}, u32[]{:S(2)}) collective-permute-start(bf16[80,384]{1,0:T(8,128)(2,1)S(1)} %collective-permute-done.9), channel_id=1, source_target_pairs={{0,480},{32,0},{64,32},{96,64},{128,96},{160,128},{192,160},{224,1... | collective-permute-start | bytes 184328 | tf_op jit(solution)/shard_map/ppermute | solution.py:106
  65.0 6.6 %collective-permute-start.12 = (bf16[80,384]{1,0:T(8,128)(2,1)S(1)}, bf16[80,384]{1,0:T(8,128)(2,1)S(1)}, u32[]{:S(2)}, u32[]{:S(2)}) collective-permute-start(bf16[80,384]{1,0:T(8,128)(2,1)S(1)} %collective-permute-done.10), channel_id=1, source_target_pairs={{0,32},{32,64},{64,96},{96,128},{128,160},{160,192},{192,224},{224... | collective-permute-start | bytes 184328 | tf_op jit(solution)/shard_map/ppermute | solution.py:103
  66.9 6.6 %collective-permute-start.13 = (bf16[80,384]{1,0:T(8,128)(2,1)S(1)}, bf16[80,384]{1,0:T(8,128)(2,1)S(1)}, u32[]{:S(2)}, u32[]{:S(2)}) collective-permute-start(bf16[80,384]{1,0:T(8,128)(2,1)S(1)} %collective-permute-done.11), channel_id=1, source_target_pairs={{0,480},{32,0},{64,32},{96,64},{128,96},{160,128},{192,160},{224,1... | collective-permute-start | bytes 184328 | tf_op jit(solution)/shard_map/ppermute | solution.py:106
  71.6 6.6 %collective-permute-start.14 = (bf16[40,384]{1,0:T(8,128)(2,1)S(1)}, bf16[40,384]{1,0:T(8,128)(2,1)S(1)}, u32[]{:S(2)}, u32[]{:S(2)}) collective-permute-start(bf16[40,384]{1,0:T(8,128)(2,1)S(1)} %slice.129), channel_id=1, source_target_pairs={{0,32},{32,64},{64,96},{96,128},{128,160},{160,192},{192,224},{224... | collective-permute-start | bytes 92168 | tf_op jit(solution)/shard_map/ppermute | solution.py:100
  73.5 5.6 %collective-permute-start.15 = (bf16[40,384]{1,0:T(8,128)(2,1)S(1)}, bf16[40,384]{1,0:T(8,128)(2,1)S(1)}, u32[]{:S(2)}, u32[]{:S(2)}) collective-permute-start(bf16[40,384]{1,0:T(8,128)(2,1)S(1)} %slice.130), channel_id=1, source_target_pairs={{0,480},{32,0},{64,32},{96,64},{128,96},{160,128},{192,160},{224,1... | collective-permute-start | bytes 92168 | tf_op jit(solution)/shard_map/ppermute | solution.py:101
  79.1 19.0 %collective-permute-start.17 = (bf16[16,80,384]{2,1,0:T(8,128)(2,1)S(1)}, bf16[16,80,384]{2,1,0:T(8,128)(2,1)S(1)}, u32[]{:S(2)}, u32[]{:S(2)}) collective-permute-start(bf16[16,80,384]{2,1,0:T(8,128)(2,1)S(1)} %bitcast_dynamic-update-slice_fusion.20), channel_id=1, source_target_pairs={{0,24},{8,0},{16,8},{24,16},{1,25},{9,1},{17,9},{25,17},{2,26},{10... | collective-permute-start | bytes 2949128 | tf_op jit(solution)/shard_map/ppermute | solution.py:106
  83.5 20.0 %collective-permute-start.16 = (bf16[16,80,384]{2,1,0:T(8,128)(2,1)S(1)}, bf16[16,80,384]{2,1,0:T(8,128)(2,1)S(1)}, u32[]{:S(2)}, u32[]{:S(2)}) collective-permute-start(bf16[16,80,384]{2,1,0:T(8,128)(2,1)S(1)} %bitcast_dynamic-update-slice_fusion.20), channel_id=1, source_target_pairs={{0,8},{8,16},{16,24},{24,0},{1,9},{9,17},{17,25},{25,1},{2,10},{10... | collective-permute-start | bytes 2949128 | tf_op jit(solution)/shard_map/ppermute | solution.py:103
  98.1 17.3 %collective-permute-start.19 = (bf16[8,80,384]{2,1,0:T(8,128)(2,1)S(1)}, bf16[8,80,384]{2,1,0:T(8,128)(2,1)S(1)}, u32[]{:S(2)}, u32[]{:S(2)}) collective-permute-start(bf16[8,80,384]{2,1,0:T(8,128)(2,1)S(1)} %slice.132), channel_id=1, source_target_pairs={{0,24},{8,0},{16,8},{24,16},{1,25},{9,1},{17,9},{25,17},{2,26},{10... | collective-permute-start | bytes 1474568 | tf_op jit(solution)/shard_map/ppermute | solution.py:101
  103.5 11.8 %collective-permute-start.18 = (bf16[8,80,384]{2,1,0:T(8,128)(2,1)S(1)}, bf16[8,80,384]{2,1,0:T(8,128)(2,1)S(1)}, u32[]{:S(2)}, u32[]{:S(2)}) collective-permute-start(bf16[8,80,384]{2,1,0:T(8,128)(2,1)S(1)} %slice.131), channel_id=1, source_target_pairs={{0,8},{8,16},{16,24},{24,0},{1,9},{9,17},{17,25},{25,1},{2,10},{10... | collective-permute-start | bytes 1474568 | tf_op jit(solution)/shard_map/ppermute | solution.py:100
  121.4 1.6 copy-start.3
  125.4 25.5 %all-to-all-start = ((f32[8,64,384]{2,1,0:T(8,128)}), f32[8,64,384]{2,1,0:T(8,128)S(1)}, u32[]{:S(2)}, u32[]{:S(2)}) async-start(f32[8,64,384]{2,1,0:T(8,128)} %fusion.50), calls=%async_computation | async-start | bytes 1572864 | tf_op jit(solution)/shard_map/all_to_all | solution.py:175
  138.7 48.0 %all-gather.5.cloned.1.call-start = ((), (), s32[]{:S(2)}) async-start(), calls=%async_computation.2 | async-start | bytes 2949120 | tf_op jit(solution)/shard_map/all_gather | solution.py:204
  156.4 1.7 copy-start.2
  186.7 5.2 %copy-start.1 = (bf16[4,2,128,256]{3,2,1,0:T(8,128)(2,1)S(1)}, bf16[4,2,128,256]{3,2,1,0:T(8,128)(2,1)}, u32[]{:S(2)}) copy-start(bf16[4,2,128,256]{3,2,1,0:T(8,128)(2,1)} %param.15) | copy-start | bytes 1572868
Sparse Core Ops, SparseCore 0:
  25.3 32.5 all-gather.2
  157.7 28.9 all-gather.4
where the time goes:
time: 200 us; the launch traced here: 199 us
  starting transfers between devices  86.2 us (43%)
  local copies, waits for them, and re-layouts  42.6 us (21%)
  waiting for transfers between devices  34.5 us (17%)
  between operations  17.2 us (9%)
  matrix products  10.5 us (5%)
  other arithmetic  7.76 us (4%)
    ppermute x8, starting transfers between devices, ring_pieces(): behind = lax.ppermute(behind, axis, backward)  41.3 us
    ppermute x8, starting transfers between devices, ring_pieces(): ahead = lax.ppermute(ahead, axis, forward)  17.8 us
    all_to_all x1, starting transfers between devices, shards(): mine = lax.all_to_all(both, 'head', 0, 1, tiled=True)  13.3 us
    ppermute x8, waiting for transfers between devices, ring_pieces(): behind = lax.ppermute(behind, axis, backward)  11.6 us
    all_to_all x1, waiting for transfers between devices, shards(): mine = lax.all_to_all(both, 'head', 0, 1, tiled=True)  10.7 us
    ppermute x2, starting transfers between devices, ring_pieces(): got.append((step, half, lax.ppermute(behind[half:], axis, backward)))  9.89 us
    ppermute x2, waiting for transfers between devices, ring_pieces(): got.append((step, 0, lax.ppermute(ahead[:half], axis, forward)))  9.46 us
    slice x3, local copies, waits for them, and re-layouts, shards(): stacked[:, part_rows:].reshape(tok_count, -1)[:, :wo_flat.shape[0]]  9.38 us
  transfers between devices with their start and end apart: 23, of which 5 were waited for; matrix products, arithmetic and copies ran while one was open for 19% of the time, Pallas kernels for 0%

commit v1 on v0

--- a/solution.py
+++ b/solution.py
@@ -172,7 +172,14 @@
     mean_square = jnp.mean(wide * wide, axis=1, keepdims=True)
     normed = (wide * lax.rsqrt(mean_square + 1e-06)).astype(jnp.bfloat16)
     both = jnp.dot(normed, proj_w, preferred_element_type=jnp.float32)
-    mine = lax.all_to_all(both, "head", 0, 1, tiled=True)
+
+    def track_the_stages_all(u):
+        carry_out = lax.psum(1, "head")
+        low = jnp.stack(jnp.split(u, carry_out, axis=0))
+        o_now = jnp.concatenate(lax.all_to_all(low, "head", 0, 0), axis=1)
+        return o_now
+
+    mine = track_the_stages_all(both)
     mine = mine.reshape(DRAFT, head_count, q_cols + kv_cols)
     q_pre = mine[:, :, :q_cols].reshape(DRAFT, HQ, HD)
     kv_pre = mine[:, :, q_cols:].reshape(DRAFT, 2 * HD)

time: 200 us -> 210 us (1.050)
  other arithmetic: 7.76 us -> 13.5 us
  local copies, waits for them, and re-layouts: 42.6 us -> 48 us
  waiting for transfers between devices: 34.5 us -> 30.7 us
    slice x3 -> x2, local copies, waits for them, and re-layouts: 9.38 us -> 5.02 us  [shards(): stacked[:, part_rows:].reshape(tok_count, -1)[:, :wo_flat.shape[0]]]
    unnamed x16 -> x59, local copies, waits for them, and re-layouts: 2.81 us -> 7.09 us
    reshape x1 -> x2, local copies, waits for them, and re-layouts: 7.12 us -> 10.9 us  [shards(): wo_cols = stacked[:, part_rows:].reshape(tok_count, -1)[:, :wo_flat.shape...]
    all_to_all x1, waiting for transfers between devices: 10.7 us -> 7.04 us  [track_the_stages_all(): o_now = jnp.concatenate(lax.all_to_all(low, 'head', 0, 0), axis=1)]
    all_gather x1 -> x0, local copies, waits for them, and re-layouts: 2.98 us -> none  [shards(): gathered = lax.all_gather(tokens, 'head', axis=1, tiled=True)]
  transfers between devices with their start and end apart: 23 -> 23, of which waited for: 5 -> 5; matrix products, arithmetic and copies ran while one was open for 19% -> 20% of each run, Pallas kernels for 0% -> 0%
where the time goes in v1:
time: 210 us; the launch traced here: 208 us
  starting transfers between devices  86.2 us (41%)
  local copies, waits for them, and re-layouts  48 us (23%)
  waiting for transfers between devices  30.7 us (15%)
  between operations  17.4 us (8%)
  other arithmetic  13.5 us (6%)
  matrix products  12.5 us (6%)
    ppermute x8, starting transfers between devices, ring_pieces(): behind = lax.ppermute(behind, axis, backward)  41.3 us
    ppermute x8, starting transfers between devices, ring_pieces(): ahead = lax.ppermute(ahead, axis, forward)  17.8 us
    all_to_all x1, starting transfers between devices, track_the_stages_all(): o_now = jnp.concatenate(lax.all_to_all(low, 'head', 0, 0), axis=1)  13.3 us
    ppermute x8, waiting for transfers between devices, ring_pieces(): behind = lax.ppermute(behind, axis, backward)  11.1 us
    reshape x2, local copies, waits for them, and re-layouts, shards(): wo_cols = stacked[:, part_rows:].reshape(tok_count, -1)[:, :wo_flat.shape...  10.9 us
    ppermute x2, starting transfers between devices, ring_pieces(): got.append((step, half, lax.ppermute(behind[half:], axis, backward)))  9.89 us
    ppermute x2, waiting for transfers between devices, ring_pieces(): got.append((step, 0, lax.ppermute(ahead[:half], axis, forward)))  9.45 us
    unnamed x59, local copies, waits for them, and re-layouts  7.09 us
  transfers between devices with their start and end apart: 23, of which 5 were waited for; matrix products, arithmetic and copies ran while one was open for 20% of the time, Pallas kernels for 0%

profile of v1, /device:TPU:1, one launch (start us, length us, event | category | flops | bytes accessed | tf_op | source)
XLA Modules:
  0.0 208.3 jit_solution(17348000472692308198)
XLA Ops:
  7.3 1.2 copy.30
  8.5 1.0 reshape.341
  11.3 4.4 %collective-permute-start = (bf16[80,384]{1,0:T(8,128)(2,1)S(1)}, bf16[80,384]{1,0:T(8,128)(2,1)S(1)}, u32[]{:S(2)}, u32[]{:S(2)}) collective-permute-start(bf16[80,384]{1,0:T(8,128)(2,1)S(1)} %get-tuple-element.6), channel_id=1, source_target_pairs={{0,32},{32,64},{64,96},{96,128},{128,160},{160,192},{192,224},{224... | collective-permute-start | bytes 184328 | tf_op jit(solution)/shard_map/ppermute | solution.py:103
  15.7 9.5 %collective-permute-start.1 = (bf16[80,384]{1,0:T(8,128)(2,1)S(1)}, bf16[80,384]{1,0:T(8,128)(2,1)S(1)}, u32[]{:S(2)}, u32[]{:S(2)}) collective-permute-start(bf16[80,384]{1,0:T(8,128)(2,1)S(1)} %get-tuple-element.6), channel_id=1, source_target_pairs={{0,480},{32,0},{64,32},{96,64},{128,96},{160,128},{192,160},{224,1... | collective-permute-start | bytes 184328 | tf_op jit(solution)/shard_map/ppermute | solution.py:106
  32.7 1.9 collective-permute-start.2
  34.6 4.6 %collective-permute-start.3 = (bf16[80,384]{1,0:T(8,128)(2,1)S(1)}, bf16[80,384]{1,0:T(8,128)(2,1)S(1)}, u32[]{:S(2)}, u32[]{:S(2)}) collective-permute-start(bf16[80,384]{1,0:T(8,128)(2,1)S(1)} %collective-permute-done.1), channel_id=1, source_target_pairs={{0,480},{32,0},{64,32},{96,64},{128,96},{160,128},{192,160},{224,1... | collective-permute-start | bytes 184328 | tf_op jit(solution)/shard_map/ppermute | solution.py:106
  39.3 1.9 collective-permute-start.4
  41.2 4.6 %collective-permute-start.5 = (bf16[80,384]{1,0:T(8,128)(2,1)S(1)}, bf16[80,384]{1,0:T(8,128)(2,1)S(1)}, u32[]{:S(2)}, u32[]{:S(2)}) collective-permute-start(bf16[80,384]{1,0:T(8,128)(2,1)S(1)} %collective-permute-done.3), channel_id=1, source_target_pairs={{0,480},{32,0},{64,32},{96,64},{128,96},{160,128},{192,160},{224,1... | collective-permute-start | bytes 184328 | tf_op jit(solution)/shard_map/ppermute | solution.py:106
  45.8 1.9 collective-permute-start.6
  47.8 4.6 %collective-permute-start.7 = (bf16[80,384]{1,0:T(8,128)(2,1)S(1)}, bf16[80,384]{1,0:T(8,128)(2,1)S(1)}, u32[]{:S(2)}, u32[]{:S(2)}) collective-permute-start(bf16[80,384]{1,0:T(8,128)(2,1)S(1)} %collective-permute-done.5), channel_id=1, source_target_pairs={{0,480},{32,0},{64,32},{96,64},{128,96},{160,128},{192,160},{224,1... | collective-permute-start | bytes 184328 | tf_op jit(solution)/shard_map/ppermute | solution.py:106
  52.4 1.9 collective-permute-start.8
  54.4 4.6 %collective-permute-start.9 = (bf16[80,384]{1,0:T(8,128)(2,1)S(1)}, bf16[80,384]{1,0:T(8,128)(2,1)S(1)}, u32[]{:S(2)}, u32[]{:S(2)}) collective-permute-start(bf16[80,384]{1,0:T(8,128)(2,1)S(1)} %collective-permute-done.7), channel_id=1, source_target_pairs={{0,480},{32,0},{64,32},{96,64},{128,96},{160,128},{192,160},{224,1... | collective-permute-start | bytes 184328 | tf_op jit(solution)/shard_map/ppermute | solution.py:106
  59.0 1.9 collective-permute-start.10
  60.9 4.6 %collective-permute-start.11 = (bf16[80,384]{1,0:T(8,128)(2,1)S(1)}, bf16[80,384]{1,0:T(8,128)(2,1)S(1)}, u32[]{:S(2)}, u32[]{:S(2)}) collective-permute-start(bf16[80,384]{1,0:T(8,128)(2,1)S(1)} %collective-permute-done.9), channel_id=1, source_target_pairs={{0,480},{32,0},{64,32},{96,64},{128,96},{160,128},{192,160},{224,1... | collective-permute-start | bytes 184328 | tf_op jit(solution)/shard_map/ppermute | solution.py:106
  65.6 1.9 collective-permute-start.12
  67.5 4.6 %collective-permute-start.13 = (bf16[80,384]{1,0:T(8,128)(2,1)S(1)}, bf16[80,384]{1,0:T(8,128)(2,1)S(1)}, u32[]{:S(2)}, u32[]{:S(2)}) collective-permute-start(bf16[80,384]{1,0:T(8,128)(2,1)S(1)} %collective-permute-done.11), channel_id=1, source_target_pairs={{0,480},{32,0},{64,32},{96,64},{128,96},{160,128},{192,160},{224,1... | collective-permute-start | bytes 184328 | tf_op jit(solution)/shard_map/ppermute | solution.py:106
  72.2 1.9 collective-permute-start.14
  74.1 4.6 %collective-permute-start.15 = (bf16[40,384]{1,0:T(8,128)(2,1)S(1)}, bf16[40,384]{1,0:T(8,128)(2,1)S(1)}, u32[]{:S(2)}, u32[]{:S(2)}) collective-permute-start(bf16[40,384]{1,0:T(8,128)(2,1)S(1)} %slice.130), channel_id=1, source_target_pairs={{0,480},{32,0},{64,32},{96,64},{128,96},{160,128},{192,160},{224,1... | collective-permute-start | bytes 92168 | tf_op jit(solution)/shard_map/ppermute | solution.py:101
  78.8 0.9 collective-permute-done.15
  79.7 4.4 %collective-permute-start.17 = (bf16[16,80,384]{2,1,0:T(8,128)(2,1)S(1)}, bf16[16,80,384]{2,1,0:T(8,128)(2,1)S(1)}, u32[]{:S(2)}, u32[]{:S(2)}) collective-permute-start(bf16[16,80,384]{2,1,0:T(8,128)(2,1)S(1)} %bitcast_dynamic-update-slice_fusion.20), channel_id=1, source_target_pairs={{0,24},{8,0},{16,8},{24,16},{1,25},{9,1},{17,9},{25,17},{2,26},{10... | collective-permute-start | bytes 2949128 | tf_op jit(solution)/shard_map/ppermute | solution.py:106
  84.1 1.9 collective-permute-start.16
  87.6 11.0 %collective-permute-done.17 = bf16[16,80,384]{2,1,0:T(8,128)(2,1)S(1)} collective-permute-done((bf16[16,80,384]{2,1,0:T(8,128)(2,1)S(1)}, bf16[16,80,384]{2,1,0:T(8,128)(2,1)S(1)}, u32[]{:S(2)}, u32[]{:S(2)}) %collective-permute-start.17) | collective-permute-done | bytes 983072 | tf_op jit(solution)/shard_map/ppermute | solution.py:106
  98.7 5.3 %collective-permute-start.19 = (bf16[8,80,384]{2,1,0:T(8,128)(2,1)S(1)}, bf16[8,80,384]{2,1,0:T(8,128)(2,1)S(1)}, u32[]{:S(2)}, u32[]{:S(2)}) collective-permute-start(bf16[8,80,384]{2,1,0:T(8,128)(2,1)S(1)} %slice.132), channel_id=1, source_target_pairs={{0,24},{8,0},{16,8},{24,16},{1,25},{9,1},{17,9},{25,17},{2,26},{10... | collective-permute-start | bytes 1474568 | tf_op jit(solution)/shard_map/ppermute | solution.py:101
  104.1 1.9 collective-permute-start.18
  106.5 9.5 %collective-permute-done.18 = bf16[8,80,384]{2,1,0:T(8,128)(2,1)S(1)} collective-permute-done((bf16[8,80,384]{2,1,0:T(8,128)(2,1)S(1)}, bf16[8,80,384]{2,1,0:T(8,128)(2,1)S(1)}, u32[]{:S(2)}, u32[]{:S(2)}) %collective-permute-start.18) | collective-permute-done | bytes 491552 | tf_op jit(solution)/shard_map/ppermute | solution.py:100
  116.1 1.7 fusion.55
  117.9 2.5 %fusion = f32[512]{0:T(512)S(1)} fusion(bf16[512,2560]{0,1:T(8,128)(2,1)} %all-gather.3.cloned.1.call-done), kind=kLoop, calls=%fused_computation.4 | loop fusion | flops 3931648 | bytes 2623488 | tf_op jit(solution)/shard_map/reduce_sum | solution.py:172
  120.4 3.1 %fusion.2 = f32[512,384]{1,0:T(8,128)S(1)} fusion(bf16[2560,384]{1,0:T(8,128)(2,1)} %bitcast.165, bf16[512,2560]{0,1:T(8,128)(2,1)S(1)} %copy-done.1, f32[512]{0:T(512)S(1)} %add_rsqrt_fusion), kind=kOutput, calls=%fused_computation.6 | convolution fusion | flops 1010565120 | bytes 5376000 | tf_op jit(solution)/shard_map/dot_general | solution.py:174
  128.7 13.3 %all-to-all-start = ((f32[8,64,384]{2,1,0:T(8,128)}), f32[8,64,384]{2,1,0:T(8,128)S(1)}, u32[]{:S(2)}, u32[]{:S(2)}) async-start(f32[8,64,384]{2,1,0:T(8,128)} %fusion.23), calls=%async_computation | async-start | bytes 1572864 | tf_op jit(solution)/shard_map/all_to_all | solution.py:179
  143.2 1.4 gather_fusion
  144.6 1.2 add_add_fusion
  147.1 7.0 %all-to-all-done = f32[8,64,384]{2,1,0:T(8,128)S(1)} async-done(((f32[8,64,384]{2,1,0:T(8,128)}), f32[8,64,384]{2,1,0:T(8,128)S(1)}, u32[]{:S(2)}, u32[]{:S(2)}) %all-to-all-start) | async-done | bytes 786464 | tf_op jit(solution)/shard_map/all_to_all | solution.py:179
  155.2 0.9 convert.35
  156.7 1.7 convolution_convert_fusion
  158.4 1.3 copy.35
  159.8 1.6 reshape.346
  162.9 1.0 fusion.16
  166.0 1.2 fusion.8
  167.2 3.8 %copy.48 = bf16[64,40,384]{0,2,1:T(8,128)(2,1)} copy(bf16[64,40,384]{2,1,0:T(8,128)(2,1)S(1)} %get-tuple-element.7) | data formatting | bytes 3932160 | tf_op jit(solution)/shard_map/reshape | solution.py:165
  171.0 3.3 %slice.145 = bf16[64,12800]{0,1:T(8,128)(2,1)} slice(bf16[64,15360]{0,1:T(8,128)(2,1)} %bitcast.162), slice={[0:64], [0:12800]} | slice | bytes 3276800 | tf_op jit(solution)/shard_map/slice | solution.py:164
  174.3 7.1 %reshape.352 = bf16[64,2560,5]{0,2,1:T(8,128)(2,1)} reshape(bf16[64,12800]{0,1:T(8,128)(2,1)} %slice.145) | data formatting | bytes 3276800 | tf_op jit(solution)/shard_map/reshape | solution.py:166
  181.5 7.0 %copy.43 = bf16[2560,64,5]{0,2,1:T(8,128)(2,1)S(1)} copy(bf16[2560,64,5]{1,2,0:T(8,128)(2,1)} %bitcast.160) | data formatting | bytes 3276800 | tf_op jit(solution)/shard_map/transpose | solution.py:167
  188.5 3.1 %reshape_reshape.3 = bf16[10,256,320]{1,0,2:T(8,128)(2,1)} reshape(bf16[2560,64,5]{0,2,1:T(8,128)(2,1)S(1)} %copy.43) | data formatting | bytes 3276800 | tf_op jit(solution)/shard_map/reshape;reshape | solution.py:214
  191.6 1.6 gather_fusion.1
  193.2 0.9 broadcast_select_fusion
  194.2 2.2 %all-gather.5.cloned.1.call-done = bf16[10,512,256]{2,1,0:T(8,128)(2,1)} async-done(((bf16[10,64,256]{2,1,0:T(8,128)(2,1)}), bf16[10,512,256]{2,1,0:T(8,128)(2,1)}) %all-gather.5.cloned.1.call-update) | async-done | bytes 2621456 | tf_op jit(solution)/shard_map/all_gather | solution.py:211
  196.3 3.9 %fusion.60 = (bf16[10,512,320]{1,2,0:T(8,128)(2,1)S(1)}, f32[10,512,320]{1,2,0:T(8,128)S(1)}) fusion(bf16[10,512,256]{2,1,0:T(8,128)(2,1)} %all-gather.5.cloned.1.call-done, bf16[10,256,320]{1,0,2:T(8,128)(2,1)} %reshape_reshape.3), kind=kOutput, calls=%fused_computation.149 | convolution fusion | flops 840499200 | bytes 14090240 | tf_op jit(solution)/shard_map/dot_general | solution.py:212
  200.2 1.2 fusion.17
  (157 shorter events, 22.3 us)
Async XLA Ops:
  7.2 136.0 %copy-start = (bf16[4,2,128,256]{3,2,1,0:T(8,128)(2,1)S(1)}, bf16[4,2,128,256]{3,2,1,0:T(8,128)(2,1)}, u32[]{:S(2)}) copy-start(bf16[4,2,128,256]{3,2,1,0:T(8,128)(2,1)} %param.15) | copy-start | bytes 1572868
  7.2 18.2 %copy-start.23 = (s32[8]{0:T(128)S(1)}, s32[8]{0:T(128)}, u32[]{:S(2)}) copy-start(s32[8]{0:T(128)} %param.19) | copy-start | bytes 100
  7.2 20.1 %copy-start.24 = (s32[8]{0:T(128)S(1)}, s32[8]{0:T(128)}, u32[]{:S(2)}) copy-start(s32[8]{0:T(128)} %param.18) | copy-start | bytes 100
  7.2 21.4 %copy-start.16 = (s32[8,4]{0,1:T(4,128)S(1)}, s32[8,4]{0,1:T(4,128)}, u32[]{:S(2)}) copy-start(s32[8,4]{0,1:T(4,128)} %param.16) | copy-start | bytes 388
  7.2 110.6 %all-gather.3.cloned.1.call-start = ((), (), s32[]{:S(2)}) async-start(), calls=%async_computation.1 | async-start | bytes 2949120 | tf_op jit(solution)/shard_map/all_gather | solution.py:170
  11.3 21.3 %collective-permute-start = (bf16[80,384]{1,0:T(8,128)(2,1)S(1)}, bf16[80,384]{1,0:T(8,128)(2,1)S(1)}, u32[]{:S(2)}, u32[]{:S(2)}) collective-permute-start(bf16[80,384]{1,0:T(8,128)(2,1)S(1)} %get-tuple-element.6), channel_id=1, source_target_pairs={{0,32},{32,64},{64,96},{96,128},{128,160},{160,192},{192,224},{224... | collective-permute-start | bytes 184328 | tf_op jit(solution)/shard_map/ppermute | solution.py:103
  15.7 18.9 %collective-permute-start.1 = (bf16[80,384]{1,0:T(8,128)(2,1)S(1)}, bf16[80,384]{1,0:T(8,128)(2,1)S(1)}, u32[]{:S(2)}, u32[]{:S(2)}) collective-permute-start(bf16[80,384]{1,0:T(8,128)(2,1)S(1)} %get-tuple-element.6), channel_id=1, source_target_pairs={{0,480},{32,0},{64,32},{96,64},{128,96},{160,128},{192,160},{224,1... | collective-permute-start | bytes 184328 | tf_op jit(solution)/shard_map/ppermute | solution.py:106
  28.9 3.8 %copy-start.20 = (s32[4]{0:T(128)}, s32[4]{0:T(128)S(1)}, u32[]{:S(2)}) copy-start(s32[4]{0:T(128)S(1)} %select_reduce_fusion) | copy-start | bytes 52
  30.1 57.3 %copy-start.9 = (s32[512]{0:T(512)}, s32[512]{0:T(512)S(1)}, u32[]{:S(2)}) copy-start(s32[512]{0:T(512)S(1)} %iota_subtract_fusion) | copy-start | bytes 6148
  32.7 6.6 %collective-permute-start.2 = (bf16[80,384]{1,0:T(8,128)(2,1)S(1)}, bf16[80,384]{1,0:T(8,128)(2,1)S(1)}, u32[]{:S(2)}, u32[]{:S(2)}) collective-permute-start(bf16[80,384]{1,0:T(8,128)(2,1)S(1)} %collective-permute-done), channel_id=1, source_target_pairs={{0,32},{32,64},{64,96},{96,128},{128,160},{160,192},{192,224},{224... | collective-permute-start | bytes 184328 | tf_op jit(solution)/shard_map/ppermute | solution.py:103
  34.6 6.6 %collective-permute-start.3 = (bf16[80,384]{1,0:T(8,128)(2,1)S(1)}, bf16[80,384]{1,0:T(8,128)(2,1)S(1)}, u32[]{:S(2)}, u32[]{:S(2)}) collective-permute-start(bf16[80,384]{1,0:T(8,128)(2,1)S(1)} %collective-permute-done.1), channel_id=1, source_target_pairs={{0,480},{32,0},{64,32},{96,64},{128,96},{160,128},{192,160},{224,1... | collective-permute-start | bytes 184328 | tf_op jit(solution)/shard_map/ppermute | solution.py:106
  39.3 6.6 %collective-permute-start.4 = (bf16[80,384]{1,0:T(8,128)(2,1)S(1)}, bf16[80,384]{1,0:T(8,128)(2,1)S(1)}, u32[]{:S(2)}, u32[]{:S(2)}) collective-permute-start(bf16[80,384]{1,0:T(8,128)(2,1)S(1)} %collective-permute-done.2), channel_id=1, source_target_pairs={{0,32},{32,64},{64,96},{96,128},{128,160},{160,192},{192,224},{224... | collective-permute-start | bytes 184328 | tf_op jit(solution)/shard_map/ppermute | solution.py:103
  41.2 6.6 %collective-permute-start.5 = (bf16[80,384]{1,0:T(8,128)(2,1)S(1)}, bf16[80,384]{1,0:T(8,128)(2,1)S(1)}, u32[]{:S(2)}, u32[]{:S(2)}) collective-permute-start(bf16[80,384]{1,0:T(8,128)(2,1)S(1)} %collective-permute-done.3), channel_id=1, source_target_pairs={{0,480},{32,0},{64,32},{96,64},{128,96},{160,128},{192,160},{224,1... | collective-permute-start | bytes 184328 | tf_op jit(solution)/shard_map/ppermute | solution.py:106
  45.8 6.6 %collective-permute-start.6 = (bf16[80,384]{1,0:T(8,128)(2,1)S(1)}, bf16[80,384]{1,0:T(8,128)(2,1)S(1)}, u32[]{:S(2)}, u32[]{:S(2)}) collective-permute-start(bf16[80,384]{1,0:T(8,128)(2,1)S(1)} %collective-permute-done.4), channel_id=1, source_target_pairs={{0,32},{32,64},{64,96},{96,128},{128,160},{160,192},{192,224},{224... | collective-permute-start | bytes 184328 | tf_op jit(solution)/shard_map/ppermute | solution.py:103
  47.8 6.6 %collective-permute-start.7 = (bf16[80,384]{1,0:T(8,128)(2,1)S(1)}, bf16[80,384]{1,0:T(8,128)(2,1)S(1)}, u32[]{:S(2)}, u32[]{:S(2)}) collective-permute-start(bf16[80,384]{1,0:T(8,128)(2,1)S(1)} %collective-permute-done.5), channel_id=1, source_target_pairs={{0,480},{32,0},{64,32},{96,64},{128,96},{160,128},{192,160},{224,1... | collective-permute-start | bytes 184328 | tf_op jit(solution)/shard_map/ppermute | solution.py:106
  52.4 6.6 %collective-permute-start.8 = (bf16[80,384]{1,0:T(8,128)(2,1)S(1)}, bf16[80,384]{1,0:T(8,128)(2,1)S(1)}, u32[]{:S(2)}, u32[]{:S(2)}) collective-permute-start(bf16[80,384]{1,0:T(8,128)(2,1)S(1)} %collective-permute-done.6), channel_id=1, source_target_pairs={{0,32},{32,64},{64,96},{96,128},{128,160},{160,192},{192,224},{224... | collective-permute-start | bytes 184328 | tf_op jit(solution)/shard_map/ppermute | solution.py:103
  54.4 6.6 %collective-permute-start.9 = (bf16[80,384]{1,0:T(8,128)(2,1)S(1)}, bf16[80,384]{1,0:T(8,128)(2,1)S(1)}, u32[]{:S(2)}, u32[]{:S(2)}) collective-permute-start(bf16[80,384]{1,0:T(8,128)(2,1)S(1)} %collective-permute-done.7), channel_id=1, source_target_pairs={{0,480},{32,0},{64,32},{96,64},{128,96},{160,128},{192,160},{224,1... | collective-permute-start | bytes 184328 | tf_op jit(solution)/shard_map/ppermute | solution.py:106
  59.0 6.6 %collective-permute-start.10 = (bf16[80,384]{1,0:T(8,128)(2,1)S(1)}, bf16[80,384]{1,0:T(8,128)(2,1)S(1)}, u32[]{:S(2)}, u32[]{:S(2)}) collective-permute-start(bf16[80,384]{1,0:T(8,128)(2,1)S(1)} %collective-permute-done.8), channel_id=1, source_target_pairs={{0,32},{32,64},{64,96},{96,128},{128,160},{160,192},{192,224},{224... | collective-permute-start | bytes 184328 | tf_op jit(solution)/shard_map/ppermute | solution.py:103
  60.9 6.6 %collective-permute-start.11 = (bf16[80,384]{1,0:T(8,128)(2,1)S(1)}, bf16[80,384]{1,0:T(8,128)(2,1)S(1)}, u32[]{:S(2)}, u32[]{:S(2)}) collective-permute-start(bf16[80,384]{1,0:T(8,128)(2,1)S(1)} %collective-permute-done.9), channel_id=1, source_target_pairs={{0,480},{32,0},{64,32},{96,64},{128,96},{160,128},{192,160},{224,1... | collective-permute-start | bytes 184328 | tf_op jit(solution)/shard_map/ppermute | solution.py:106
  65.6 6.6 %collective-permute-start.12 = (bf16[80,384]{1,0:T(8,128)(2,1)S(1)}, bf16[80,384]{1,0:T(8,128)(2,1)S(1)}, u32[]{:S(2)}, u32[]{:S(2)}) collective-permute-start(bf16[80,384]{1,0:T(8,128)(2,1)S(1)} %collective-permute-done.10), channel_id=1, source_target_pairs={{0,32},{32,64},{64,96},{96,128},{128,160},{160,192},{192,224},{224... | collective-permute-start | bytes 184328 | tf_op jit(solution)/shard_map/ppermute | solution.py:103
  67.5 6.6 %collective-permute-start.13 = (bf16[80,384]{1,0:T(8,128)(2,1)S(1)}, bf16[80,384]{1,0:T(8,128)(2,1)S(1)}, u32[]{:S(2)}, u32[]{:S(2)}) collective-permute-start(bf16[80,384]{1,0:T(8,128)(2,1)S(1)} %collective-permute-done.11), channel_id=1, source_target_pairs={{0,480},{32,0},{64,32},{96,64},{128,96},{160,128},{192,160},{224,1... | collective-permute-start | bytes 184328 | tf_op jit(solution)/shard_map/ppermute | solution.py:106
  72.2 6.6 %collective-permute-start.14 = (bf16[40,384]{1,0:T(8,128)(2,1)S(1)}, bf16[40,384]{1,0:T(8,128)(2,1)S(1)}, u32[]{:S(2)}, u32[]{:S(2)}) collective-permute-start(bf16[40,384]{1,0:T(8,128)(2,1)S(1)} %slice.129), channel_id=1, source_target_pairs={{0,32},{32,64},{64,96},{96,128},{128,160},{160,192},{192,224},{224... | collective-permute-start | bytes 92168 | tf_op jit(solution)/shard_map/ppermute | solution.py:100
  74.1 5.6 %collective-permute-start.15 = (bf16[40,384]{1,0:T(8,128)(2,1)S(1)}, bf16[40,384]{1,0:T(8,128)(2,1)S(1)}, u32[]{:S(2)}, u32[]{:S(2)}) collective-permute-start(bf16[40,384]{1,0:T(8,128)(2,1)S(1)} %slice.130), channel_id=1, source_target_pairs={{0,480},{32,0},{64,32},{96,64},{128,96},{160,128},{192,160},{224,1... | collective-permute-start | bytes 92168 | tf_op jit(solution)/shard_map/ppermute | solution.py:101
  79.7 19.0 %collective-permute-start.17 = (bf16[16,80,384]{2,1,0:T(8,128)(2,1)S(1)}, bf16[16,80,384]{2,1,0:T(8,128)(2,1)S(1)}, u32[]{:S(2)}, u32[]{:S(2)}) collective-permute-start(bf16[16,80,384]{2,1,0:T(8,128)(2,1)S(1)} %bitcast_dynamic-update-slice_fusion.20), channel_id=1, source_target_pairs={{0,24},{8,0},{16,8},{24,16},{1,25},{9,1},{17,9},{25,17},{2,26},{10... | collective-permute-start | bytes 2949128 | tf_op jit(solution)/shard_map/ppermute | solution.py:106
  84.1 20.0 %collective-permute-start.16 = (bf16[16,80,384]{2,1,0:T(8,128)(2,1)S(1)}, bf16[16,80,384]{2,1,0:T(8,128)(2,1)S(1)}, u32[]{:S(2)}, u32[]{:S(2)}) collective-permute-start(bf16[16,80,384]{2,1,0:T(8,128)(2,1)S(1)} %bitcast_dynamic-update-slice_fusion.20), channel_id=1, source_target_pairs={{0,8},{8,16},{16,24},{24,0},{1,9},{9,17},{17,25},{25,1},{2,10},{10... | collective-permute-start | bytes 2949128 | tf_op jit(solution)/shard_map/ppermute | solution.py:103
  86.0 1.6 copy-start.11
  86.3 1.4 copy-start.13
  98.7 17.3 %collective-permute-start.19 = (bf16[8,80,384]{2,1,0:T(8,128)(2,1)S(1)}, bf16[8,80,384]{2,1,0:T(8,128)(2,1)S(1)}, u32[]{:S(2)}, u32[]{:S(2)}) collective-permute-start(bf16[8,80,384]{2,1,0:T(8,128)(2,1)S(1)} %slice.132), channel_id=1, source_target_pairs={{0,24},{8,0},{16,8},{24,16},{1,25},{9,1},{17,9},{25,17},{2,26},{10... | collective-permute-start | bytes 1474568 | tf_op jit(solution)/shard_map/ppermute | solution.py:101
  104.1 11.8 %collective-permute-start.18 = (bf16[8,80,384]{2,1,0:T(8,128)(2,1)S(1)}, bf16[8,80,384]{2,1,0:T(8,128)(2,1)S(1)}, u32[]{:S(2)}, u32[]{:S(2)}) collective-permute-start(bf16[8,80,384]{2,1,0:T(8,128)(2,1)S(1)} %slice.131), channel_id=1, source_target_pairs={{0,8},{8,16},{16,24},{24,0},{1,9},{9,17},{17,25},{25,1},{2,10},{10... | collective-permute-start | bytes 1474568 | tf_op jit(solution)/shard_map/ppermute | solution.py:100
  117.9 2.5 %copy-start.1 = (bf16[512,2560]{0,1:T(8,128)(2,1)S(1)}, bf16[512,2560]{0,1:T(8,128)(2,1)}, u32[]{:S(2)}) copy-start(bf16[512,2560]{0,1:T(8,128)(2,1)} %all-gather.3.cloned.1.call-done) | copy-start | bytes 7864324
  128.7 25.5 %all-to-all-start = ((f32[8,64,384]{2,1,0:T(8,128)}), f32[8,64,384]{2,1,0:T(8,128)S(1)}, u32[]{:S(2)}, u32[]{:S(2)}) async-start(f32[8,64,384]{2,1,0:T(8,128)} %fusion.23), calls=%async_computation | async-start | bytes 1572864 | tf_op jit(solution)/shard_map/all_to_all | solution.py:179
  142.0 54.4 %all-gather.5.cloned.1.call-start = ((), (), s32[]{:S(2)}) async-start(), calls=%async_computation.2 | async-start | bytes 2949120 | tf_op jit(solution)/shard_map/all_gather | solution.py:211
  156.1 0.6 copy-start.5
  161.3 0.9 copy-start.4
  161.4 0.9 copy-start.15
  161.4 0.9 copy-start.19
  161.4 1.1 copy-start.10
  161.4 1.1 copy-start.12
  161.4 1.1 copy-start.14
  161.4 1.4 copy-start.2
  161.4 1.4 copy-start.3
  161.4 1.4 copy-start.18
  161.4 1.4 copy-start.22
  162.9 1.3 copy-start.8
  163.8 0.8 copy-start.7
  164.2 1.5 copy-start.6
  166.0 1.2 copy-start.17
  166.0 1.2 copy-start.21
Sparse Core Ops, SparseCore 0:
  25.3 32.5 all-gather.2
  167.3 28.9 all-gather.4
